TPU v7x, 512 devices: a whole 4x8x8 slice. The times are simulated.
512 devices in a mesh: depth: 16 (over x_hi, y), scan: 32 (over z, x_lo, core).
Axes of the slice: x: 4 (x_hi: 2, x_lo: 2; x = x_hi * 2 + x_lo), y: 8, z: 8, core: 2. Of those that a mesh axis runs over, the one named last changes fastest.
Arguments:
- object_slice: bfloat16 [2, 4, 512, 2048], P(None, None, 'depth', 'scan'), may hold values from -4 to 4
- probe_field: bfloat16 [2, 512, 512], replicated, may hold values from -2 to 2
- offsets: int32 [64, 2], replicated, may hold values from 0 to 1536
- assignment: int32 [64], P('scan'), may hold values from 0 to 63, each once
- intensities: float32 [64, 512, 512], P('scan', 'depth'), may hold values from 0 to 3
Outputs:
- object_grad: float32 [2, 4, 512, 2048], P(None, None, 'depth', 'scan')
- probe_grad: float32 [2, 512, 512], P(None, 'depth')
Inputs may be any that keep to these rules, and one draw needn't show every extreme that they name: `offsets`: each window lies inside the object window. `assignment`: every position stands in exactly one slot; slots s * 2 to s * 2 + 1 lie on index s of scan.
All inputs are finite; a program needn't handle non-finite values.
Results may differ from a plain program's by a relative error of at most 0.0003.
Values may be sent and summed in bfloat16 or wider, within the bound.
No kernel may reach another device: no remote copies, remote signals or barrier semaphores. Data moves between devices by JAX's collectives and lax.ppermute only.
A program may use at most 64 MiB of HBM per device.

v0:
```python
import math
import jax
import jax.numpy as jnp
from jax import lax
from jax.sharding import PartitionSpec as P

fresnel_scale = 4


def from_behind(block, axis, distance):
    devices = range(lax.axis_size(axis))
    route = [((i - distance) % len(devices), i) for i in devices]
    return lax.ppermute(block, axis, route)


def dft_table(size):
    index = jnp.arange(size, dtype=jnp.int32)
    turns = index[:, None] * index[None, :] % size
    angle = 2.0 * math.pi / size * turns.astype(jnp.float32)
    norm = 1.0 / math.sqrt(size)
    return (jnp.cos(angle) * norm, -jnp.sin(angle) * norm)


def chirp_phase(index, size):
    centred = index - size // 2
    period = 2 * fresnel_scale * size
    phase = centred * centred % period
    angle = math.pi / (fresnel_scale * size) * phase.astype(jnp.float32)
    return (jnp.cos(angle), jnp.sin(angle))


def contract(form, left_side, right_side):
    return jnp.einsum(
        form,
        left_side,
        right_side,
        precision=lax.Precision.HIGHEST,
        preferred_element_type=jnp.float32,
    )


def complex_mix(form, left_re, left_im, right_re, right_im):
    real_part = contract(form, left_re, right_re) - contract(form, left_im, right_im)
    imag_part = contract(form, left_re, right_im) + contract(form, left_im, right_re)
    return (real_part, imag_part)


def on_device(object_slice, probe_field, offsets, assignment, intensities):
    depth_count = lax.axis_size("depth")
    depth_index = lax.axis_index("depth")
    rows_dev = object_slice.shape[2]
    cycles = object_slice.shape[1]
    patch_side = probe_field.shape[2]
    pos_count = assignment.shape[0]
    total_pos = pos_count * lax.axis_size("scan")
    band_rows = lax.all_gather(object_slice, "scan", axis=3, tiled=True)
    full_width = band_rows.shape[3]
    flat_band = band_rows.reshape(2, cycles * rows_dev, full_width)
    position = offsets[assignment]
    top_row = position[:, 0]
    left_col = position[:, 1]
    table_re, table_im = dft_table(patch_side)
    row_ids = jnp.arange(rows_dev, dtype=jnp.int32)
    col_ids = jnp.arange(patch_side, dtype=jnp.int32)
    col_cos, col_sin = chirp_phase(col_ids, patch_side)
    zero_start = jnp.int32(0)

    def cut_tile(cycle_row, column):
        return lax.dynamic_slice(
            flat_band, (zero_start, cycle_row * rows_dev, column), (2, rows_dev, patch_side)
        )

    block_first = top_row // rows_dev
    offset_in = top_row % rows_dev
    first_block = block_first + (depth_index - block_first) % depth_count
    first_cycle = first_block // depth_count
    second_cycle = jnp.minimum(first_cycle + 1, cycles - 1)
    pair_tiles = jnp.stack(
        [jax.vmap(cut_tile)(first_cycle, left_col), jax.vmap(cut_tile)(second_cycle, left_col)], 1
    )
    levels = depth_count.bit_length() - 1
    amount = (depth_count - block_first % depth_count) % depth_count
    for level in range(levels):
        moved = from_behind(pair_tiles, "depth", 1 << level)
        taken = amount >> level & 1 == 1
        pair_tiles = jnp.where(taken[:, None, None, None, None], moved, pair_tiles)
    first_tile = pair_tiles[:, 0]
    outgoing = jnp.where(depth_index == 0, pair_tiles[:, 1], first_tile)
    following = from_behind(outgoing, "depth", depth_count - 1)
    stacked = jnp.concatenate([first_tile, following], 2)

    def take_rows(tile_pair, corner_row):
        return lax.dynamic_slice_in_dim(tile_pair, corner_row, rows_dev, 1)

    patch = jax.vmap(take_rows)(stacked, offset_in)
    patch_rows = jnp.broadcast_to(depth_index * rows_dev + row_ids[None, :], (pos_count, rows_dev))
    probe_rows = lax.dynamic_slice_in_dim(probe_field, depth_index * rows_dev, rows_dev, 1)[None]
    row_cos, row_sin = chirp_phase(patch_rows, patch_side)
    chirp_re = (
        row_cos[:, :, None] * col_cos[None, None, :] - row_sin[:, :, None] * col_sin[None, None, :]
    )
    chirp_im = (
        row_sin[:, :, None] * col_cos[None, None, :] + row_cos[:, :, None] * col_sin[None, None, :]
    )
    obj_re = patch[:, 0].astype(jnp.float32)
    obj_im = patch[:, 1].astype(jnp.float32)
    probe_re = probe_rows[:, 0].astype(jnp.float32)
    probe_im = probe_rows[:, 1].astype(jnp.float32)
    wave_re = probe_re * obj_re - probe_im * obj_im
    wave_im = probe_re * obj_im + probe_im * obj_re
    psi_re = wave_re * chirp_re - wave_im * chirp_im
    psi_im = wave_re * chirp_im + wave_im * chirp_re
    half_re, half_im = complex_mix("vk,pjk->pvj", table_re, table_im, psi_re, psi_im)
    half_re, half_im = (
        lax.all_to_all(half_re, "depth", split_axis=1, concat_axis=2, tiled=True),
        lax.all_to_all(half_im, "depth", split_axis=1, concat_axis=2, tiled=True),
    )
    far_re, far_im = complex_mix("pvj,ju->pvu", half_re, half_im, table_re, table_im)
    excess = far_re * far_re + far_im * far_im - intensities
    resid_re = excess * far_re
    resid_im = excess * far_im
    mid_re, mid_im = complex_mix("pvu,uj->pvj", resid_re, resid_im, table_re, -table_im)
    mid_re, mid_im = (
        lax.all_to_all(mid_re, "depth", split_axis=2, concat_axis=1, tiled=True),
        lax.all_to_all(mid_im, "depth", split_axis=2, concat_axis=1, tiled=True),
    )
    back_re, back_im = complex_mix("vk,pvj->pjk", table_re, -table_im, mid_re, mid_im)
    grad_re = back_re * chirp_re + back_im * chirp_im
    grad_im = back_im * chirp_re - back_re * chirp_im
    contrib = jnp.stack(
        [probe_re * grad_re + probe_im * grad_im, probe_re * grad_im - probe_im * grad_re], 1
    )
    term_re = obj_re * grad_re + obj_im * grad_im
    term_im = obj_re * grad_im - obj_im * grad_re
    grad_band = jnp.zeros((2, cycles * rows_dev, full_width), jnp.float32)

    def add_tile(band_now, tile_value, cycle_row, column):
        corner = (zero_start, cycle_row * rows_dev, column)
        current = lax.dynamic_slice(band_now, corner, (2, rows_dev, patch_side))
        return lax.dynamic_update_slice(band_now, current + tile_value, corner)

    empty_window = jnp.zeros((pos_count, 2, 2 * rows_dev, patch_side), jnp.float32)

    def place_rows(window_zero, tile_rows, corner_row):
        return lax.dynamic_update_slice_in_dim(window_zero, tile_rows, corner_row, 1)

    placed = jax.vmap(place_rows)(empty_window, contrib, offset_in)
    head_part = placed[:, :, :rows_dev]
    tail_part = placed[:, :, rows_dev:]
    returned = from_behind(tail_part, "depth", 1)
    is_first = depth_index == 0
    head_part = jnp.where(is_first, head_part, head_part + returned)
    second_part = jnp.where(is_first, returned, jnp.zeros_like(returned))
    grad_pair = jnp.stack([head_part, second_part], 1)
    amount_back = block_first % depth_count
    for level in range(levels):
        moved_back = from_behind(grad_pair, "depth", 1 << level)
        taken_back = amount_back >> level & 1 == 1
        grad_pair = jnp.where(taken_back[:, None, None, None, None], moved_back, grad_pair)
    for slot_index in range(pos_count):
        grad_band = add_tile(
            grad_band, grad_pair[slot_index, 0], first_cycle[slot_index], left_col[slot_index]
        )
        grad_band = add_tile(
            grad_band, grad_pair[slot_index, 1], second_cycle[slot_index], left_col[slot_index]
        )
    probe_sum = jnp.stack([jnp.sum(term_re, 0), jnp.sum(term_im, 0)])
    probe_grad = lax.psum(probe_sum, "scan")
    object_grad = lax.psum_scatter(
        grad_band.reshape(2, cycles, rows_dev, full_width), "scan", scatter_dimension=3, tiled=True
    )
    return (object_grad, probe_grad * total_pos ** (-0.5))


def solution(mesh):
    return jax.shard_map(
        on_device,
        mesh=mesh,
        in_specs=(P(None, None, "depth", "scan"), P(), P(), P("scan"), P("scan", "depth", None)),
        out_specs=(P(None, None, "depth", "scan"), P(None, "depth", None)),
        check_vma=False,
    )
```

profile of v0, /device:TPU:8, one launch (start us, length us, event | category | flops | bytes accessed | tf_op | source)
XLA Modules:
  0.0 748.6 jit_solution(7698439106445803496)
XLA Ops:
  11.9 73.0 %all-gather.2.cloned.1.call-done = bf16[2,4,32,2048]{2,1,0,3:T(4,128)(2,1)} async-done(((bf16[2,4,32,64]{2,1,0,3:T(4,128)(2,1)}), bf16[2,4,32,2048]{2,1,0,3:T(4,128)(2,1)}) %all-gather.2.cloned.1.call-update) | async-done | bytes 1048592 | tf_op jit(solution)/shard_map/all_gather | solution.py:56
  85.0 5.5 copy.64
  90.5 4.2 while.4
  94.8 4.2 while.3
  99.4 3.4 collective-permute-start
  102.9 6.9 collective-permute-done
  110.3 4.5 collective-permute-start.1
  114.8 9.8 %collective-permute-done.1 = bf16[2,2,2,32,512]{4,2,0,3,1:T(2,128)(2,1)S(1)} collective-permute-done((bf16[2,2,2,32,512]{4,2,0,3,1:T(2,128)(2,1)S(1)}, bf16[2,2,2,32,512]{4,2,0,3,1:T(2,128)(2,1)S(1)}, u32[]{:S(2)}, u32[]{:S(2)}) %collective-permute-start.1) | collective-permute-done | bytes 262176 | tf_op jit(solution)/shard_map/ppermute | solution.py:13
  125.3 4.8 collective-permute-start.2
  130.1 15.7 %collective-permute-done.2 = bf16[2,2,2,32,512]{4,2,0,3,1:T(2,128)(2,1)S(1)} collective-permute-done((bf16[2,2,2,32,512]{4,2,0,3,1:T(2,128)(2,1)S(1)}, bf16[2,2,2,32,512]{4,2,0,3,1:T(2,128)(2,1)S(1)}, u32[]{:S(2)}, u32[]{:S(2)}) %collective-permute-start.2) | collective-permute-done | bytes 262176 | tf_op jit(solution)/shard_map/ppermute | solution.py:13
  149.0 8.0 %collective-permute-done.3 = bf16[2,2,2,32,512]{4,2,0,3,1:T(2,128)(2,1)S(1)} collective-permute-done((bf16[2,2,2,32,512]{4,2,0,3,1:T(2,128)(2,1)S(1)}, bf16[2,2,2,32,512]{4,2,0,3,1:T(2,128)(2,1)S(1)}, u32[]{:S(2)}, u32[]{:S(2)}) %collective-permute-start.3) | collective-permute-done | bytes 262176 | tf_op jit(solution)/shard_map/ppermute | solution.py:13
  157.6 8.7 %collective-permute-start.4 = (bf16[2,2,32,512]{3,1,0,2:T(2,128)(2,1)S(1)}, bf16[2,2,32,512]{3,1,0,2:T(2,128)(2,1)S(1)}, u32[]{:S(2)}, u32[]{:S(2)}) collective-permute-start(bf16[2,2,32,512]{3,1,0,2:T(2,128)(2,1)S(1)} %broadcast_select_fusion.8), channel_id=1, source_target_pairs={{32,0},{64,32},{96,64},{128,96},{160,128},{192,160},{224,192},{256... | collective-permute-start | bytes 393224 | tf_op jit(solution)/shard_map/ppermute | solution.py:13
  170.0 5.0 fusion.27
  175.0 5.0 fusion.23
  180.0 5.2 fusion.1
  186.7 7.4 all-to-all-start
  194.0 5.0 fusion
  203.5 7.1 all-to-all-start.1
  213.1 4.8 fusion.25
  217.8 4.8 fusion.10
  224.6 4.7 convolution_add_fusion.2
  229.3 4.9 convolution_subtract_fusion.2
  234.3 4.8 fusion.7
  239.1 4.8 fusion.20
  243.9 4.8 convolution_subtract_fusion.1
  250.2 9.6 %all-to-all-start.2 = ((f32[16,1,2048]{2,1,0:T(1,128)}), f32[16,1,2048]{2,1,0:T(1,128)S(1)}, u32[]{:S(2)}, u32[]{:S(2)}) async-start(f32[16,1,2048]{2,1,0:T(1,128)} %reshape.375), calls=%async_computation.2 | async-start | bytes 262144 | tf_op jit(solution)/shard_map/all_to_all | solution.py:124
  259.8 4.7 convolution_add_fusion.1
  269.3 6.3 all-to-all-start.3
  277.7 5.0 fusion.18
  287.1 4.8 fusion.15
  291.9 4.8 convolution_add_fusion
  296.7 4.9 fusion.40
  301.8 14.5 %while.5 = (s32[]{:T(128)}, f32[2,2,64,512]{3,1,0,2:T(2,128)S(1)}, s32[2,4]{1,0:T(2,128)S(1)}, f32[2,2,32,512]{3,2,0,1:T(8,128)S(1)}, s32[]{:T(128)}, /*index=5*/s32[4]{0:T(128)S(1)}) while((s32[]{:T(128)}, f32[2,2,64,512]{3,1,0,2:T(2,128)S(1)}, s32[2,4]{1,0:T(2,128)S(1)}, f32[2,2,32,512]{3,2,0,1:T(8,128)S(1)}, s32[]{:T(128)}, ...), condition=%wide.while_cond.2, body=%wide.while_body.2.sunk | while | flops 32797 | bytes 917703 | solution.py:145
  318.9 5.6 collective-permute-done.5
  325.0 4.3 collective-permute-start.6
  329.3 9.1 %collective-permute-done.6 = f32[2,2,2,32,512]{4,2,0,3,1:T(2,128)S(1)} collective-permute-done((f32[2,2,2,32,512]{4,2,0,3,1:T(2,128)S(1)}, f32[2,2,2,32,512]{4,2,0,3,1:T(2,128)S(1)}, u32[]{:S(2)}, u32[]{:S(2)}) %collective-permute-start.6) | collective-permute-done | bytes 524320 | tf_op jit(solution)/shard_map/ppermute | solution.py:13
  338.8 4.0 collective-permute-start.7
  342.8 18.4 %collective-permute-done.7 = f32[2,2,2,32,512]{4,2,0,3,1:T(2,128)S(1)} collective-permute-done((f32[2,2,2,32,512]{4,2,0,3,1:T(2,128)S(1)}, f32[2,2,2,32,512]{4,2,0,3,1:T(2,128)S(1)}, u32[]{:S(2)}, u32[]{:S(2)}) %collective-permute-start.7) | collective-permute-done | bytes 524320 | tf_op jit(solution)/shard_map/ppermute | solution.py:13
  361.6 4.7 collective-permute-start.8
  366.3 20.3 %collective-permute-done.8 = f32[2,2,2,32,512]{4,2,0,3,1:T(2,128)S(1)} collective-permute-done((f32[2,2,2,32,512]{4,2,0,3,1:T(2,128)S(1)}, f32[2,2,2,32,512]{4,2,0,3,1:T(2,128)S(1)}, u32[]{:S(2)}, u32[]{:S(2)}) %collective-permute-start.8) | collective-permute-done | bytes 524320 | tf_op jit(solution)/shard_map/ppermute | solution.py:13
  401.8 6.2 dynamic_update_slice.12
  409.1 6.2 dynamic_update_slice.13
  416.4 6.1 dynamic_update_slice.14
  423.7 6.1 dynamic_update_slice.15
  429.8 6.1 copy.84
  436.0 8.6 %reshape.365 = f32[2048,256]{1,0:T(8,128)} reshape(f32[2048,2,4,32]{3,2,1,0:T(4,128)} %bitcast.195) | data formatting | bytes 4194304
  444.6 169.5 %all-reduce.2.cloned.1.call-done = f32[2,32,512]{2,1,0:T(8,128)} async-done(((f32[2,32,512]{2,1,0:T(8,128)}), f32[2,32,512]{2,1,0:T(8,128)}) %all-reduce.2.cloned.1.call-update) | async-done | bytes 131088 | tf_op jit(solution)/shard_map/psum | solution.py:168
  615.6 124.2 %reduce-scatter.4.cloned.1.call-done = f32[64,256]{1,0:T(8,128)} async-done(((f32[2048,256]{1,0:T(8,128)}), f32[64,256]{1,0:T(8,128)}) %reduce-scatter.4.cloned.1.call-update) | async-done | bytes 65552
  (131 shorter events, 78.9 us)
Async XLA Ops:
  7.2 107.7 %copy-start = (bf16[2,512,512]{2,1,0:T(8,128)(2,1)S(1)}, bf16[2,512,512]{2,1,0:T(8,128)(2,1)}, u32[]{:S(2)}) copy-start(bf16[2,512,512]{2,1,0:T(8,128)(2,1)} %param.6) | copy-start | bytes 3145732
  7.2 77.8 %all-gather.2.cloned.1.call-start = ((), (), s32[]{:S(2)}) async-start(), calls=%async_computation.5 | async-start | bytes 4325376 | tf_op jit(solution)/shard_map/all_gather | solution.py:56
  99.4 10.3 %collective-permute-start = (bf16[2,2,2,32,512]{4,2,0,3,1:T(2,128)(2,1)S(1)}, bf16[2,2,2,32,512]{4,2,0,3,1:T(2,128)(2,1)S(1)}, u32[]{:S(2)}, u32[]{:S(2)}) collective-permute-start(bf16[2,2,2,32,512]{4,2,0,3,1:T(2,128)(2,1)S(1)} %pad_maximum_fusion.1), channel_id=1, source_target_pairs={{480,0},{0,32},{32,64},{64,96},{96,128},{128,160},{160,192},{192,2... | collective-permute-start | bytes 786440 | tf_op jit(solution)/shard_map/ppermute | solution.py:13
  110.3 14.4 %collective-permute-start.1 = (bf16[2,2,2,32,512]{4,2,0,3,1:T(2,128)(2,1)S(1)}, bf16[2,2,2,32,512]{4,2,0,3,1:T(2,128)(2,1)S(1)}, u32[]{:S(2)}, u32[]{:S(2)}) collective-permute-start(bf16[2,2,2,32,512]{4,2,0,3,1:T(2,128)(2,1)S(1)} %broadcast_select_fusion.4), channel_id=1, source_target_pairs={{448,0},{480,32},{0,64},{32,96},{64,128},{96,160},{128,192},{160,2... | collective-permute-start | bytes 786440 | tf_op jit(solution)/shard_map/ppermute | solution.py:13
  125.3 20.5 %collective-permute-start.2 = (bf16[2,2,2,32,512]{4,2,0,3,1:T(2,128)(2,1)S(1)}, bf16[2,2,2,32,512]{4,2,0,3,1:T(2,128)(2,1)S(1)}, u32[]{:S(2)}, u32[]{:S(2)}) collective-permute-start(bf16[2,2,2,32,512]{4,2,0,3,1:T(2,128)(2,1)S(1)} %broadcast_select_fusion.5), channel_id=1, source_target_pairs={{384,0},{416,32},{448,64},{480,96},{0,128},{32,160},{64,192},{96,2... | collective-permute-start | bytes 786440 | tf_op jit(solution)/shard_map/ppermute | solution.py:13
  146.2 10.9 %collective-permute-start.3 = (bf16[2,2,2,32,512]{4,2,0,3,1:T(2,128)(2,1)S(1)}, bf16[2,2,2,32,512]{4,2,0,3,1:T(2,128)(2,1)S(1)}, u32[]{:S(2)}, u32[]{:S(2)}) collective-permute-start(bf16[2,2,2,32,512]{4,2,0,3,1:T(2,128)(2,1)S(1)} %broadcast_select_fusion.6), channel_id=1, source_target_pairs={{256,0},{288,32},{320,64},{352,96},{384,128},{416,160},{448,192},{... | collective-permute-start | bytes 786440 | tf_op jit(solution)/shard_map/ppermute | solution.py:13
  157.6 11.0 %collective-permute-start.4 = (bf16[2,2,32,512]{3,1,0,2:T(2,128)(2,1)S(1)}, bf16[2,2,32,512]{3,1,0,2:T(2,128)(2,1)S(1)}, u32[]{:S(2)}, u32[]{:S(2)}) collective-permute-start(bf16[2,2,32,512]{3,1,0,2:T(2,128)(2,1)S(1)} %broadcast_select_fusion.8), channel_id=1, source_target_pairs={{32,0},{64,32},{96,64},{128,96},{160,128},{192,160},{224,192},{256... | collective-permute-start | bytes 393224 | tf_op jit(solution)/shard_map/ppermute | solution.py:13
  186.7 16.9 %all-to-all-start = ((f32[16,1,2048]{2,1,0:T(1,128)}), f32[16,1,2048]{2,1,0:T(1,128)S(1)}, u32[]{:S(2)}, u32[]{:S(2)}) async-start(f32[16,1,2048]{2,1,0:T(1,128)} %reshape.369), calls=%async_computation | async-start | bytes 262144 | tf_op jit(solution)/shard_map/all_to_all | solution.py:115
  203.5 19.1 %all-to-all-start.1 = ((f32[16,1,2048]{2,1,0:T(1,128)}), f32[16,1,2048]{2,1,0:T(1,128)S(1)}, u32[]{:S(2)}, u32[]{:S(2)}) async-start(f32[16,1,2048]{2,1,0:T(1,128)} %reshape.371), calls=%async_computation.1 | async-start | bytes 262144 | tf_op jit(solution)/shard_map/all_to_all | solution.py:116
  229.3 5.0 copy-start.3
  250.2 19.1 %all-to-all-start.2 = ((f32[16,1,2048]{2,1,0:T(1,128)}), f32[16,1,2048]{2,1,0:T(1,128)S(1)}, u32[]{:S(2)}, u32[]{:S(2)}) async-start(f32[16,1,2048]{2,1,0:T(1,128)} %reshape.375), calls=%async_computation.2 | async-start | bytes 262144 | tf_op jit(solution)/shard_map/all_to_all | solution.py:124
  269.3 15.8 %all-to-all-start.3 = ((f32[16,1,2048]{2,1,0:T(1,128)}), f32[16,1,2048]{2,1,0:T(1,128)S(1)}, u32[]{:S(2)}, u32[]{:S(2)}) async-start(f32[16,1,2048]{2,1,0:T(1,128)} %reshape.373), calls=%async_computation.3 | async-start | bytes 262144 | tf_op jit(solution)/shard_map/all_to_all | solution.py:125
  275.6 338.4 %all-reduce.2.cloned.1.call-start = ((), (), s32[]{:S(2)}) async-start(), calls=%async_computation.6 | async-start | bytes 262144 | tf_op jit(solution)/shard_map/psum | solution.py:168
  296.6 5.1 copy-start.2
  316.3 8.3 %collective-permute-start.5 = (f32[2,2,32,512]{3,1,0,2:T(2,128)S(1)}, f32[2,2,32,512]{3,1,0,2:T(2,128)S(1)}, u32[]{:S(2)}, u32[]{:S(2)}) collective-permute-start(f32[2,2,32,512]{3,1,0,2:T(2,128)S(1)} %slice.75), channel_id=1, source_target_pairs={{480,0},{0,32},{32,64},{64,96},{96,128},{128,160},{160,192},{192,2... | collective-permute-start | bytes 786440 | tf_op jit(solution)/shard_map/ppermute | solution.py:13
  325.0 13.3 %collective-permute-start.6 = (f32[2,2,2,32,512]{4,2,0,3,1:T(2,128)S(1)}, f32[2,2,2,32,512]{4,2,0,3,1:T(2,128)S(1)}, u32[]{:S(2)}, u32[]{:S(2)}) collective-permute-start(f32[2,2,2,32,512]{4,2,0,3,1:T(2,128)S(1)} %pad_maximum_fusion), channel_id=1, source_target_pairs={{480,0},{0,32},{32,64},{64,96},{96,128},{128,160},{160,192},{192,2... | collective-permute-start | bytes 1572872 | tf_op jit(solution)/shard_map/ppermute | solution.py:13
  338.8 22.4 %collective-permute-start.7 = (f32[2,2,2,32,512]{4,2,0,3,1:T(2,128)S(1)}, f32[2,2,2,32,512]{4,2,0,3,1:T(2,128)S(1)}, u32[]{:S(2)}, u32[]{:S(2)}) collective-permute-start(f32[2,2,2,32,512]{4,2,0,3,1:T(2,128)S(1)} %broadcast_select_fusion), channel_id=1, source_target_pairs={{448,0},{480,32},{0,64},{32,96},{64,128},{96,160},{128,192},{160,2... | collective-permute-start | bytes 1572872 | tf_op jit(solution)/shard_map/ppermute | solution.py:13
  361.6 25.0 %collective-permute-start.8 = (f32[2,2,2,32,512]{4,2,0,3,1:T(2,128)S(1)}, f32[2,2,2,32,512]{4,2,0,3,1:T(2,128)S(1)}, u32[]{:S(2)}, u32[]{:S(2)}) collective-permute-start(f32[2,2,2,32,512]{4,2,0,3,1:T(2,128)S(1)} %broadcast_select_fusion.1), channel_id=1, source_target_pairs={{384,0},{416,32},{448,64},{480,96},{0,128},{32,160},{64,192},{96,2... | collective-permute-start | bytes 1572872 | tf_op jit(solution)/shard_map/ppermute | solution.py:13
  387.0 12.6 %collective-permute-start.9 = (f32[2,2,2,32,512]{4,2,0,3,1:T(2,128)S(1)}, f32[2,2,2,32,512]{4,2,0,3,1:T(2,128)S(1)}, u32[]{:S(2)}, u32[]{:S(2)}) collective-permute-start(f32[2,2,2,32,512]{4,2,0,3,1:T(2,128)S(1)} %broadcast_select_fusion.2), channel_id=1, source_target_pairs={{256,0},{288,32},{320,64},{352,96},{384,128},{416,160},{448,192},{... | collective-permute-start | bytes 1572872 | tf_op jit(solution)/shard_map/ppermute | solution.py:13
  397.2 342.6 %reduce-scatter.4.cloned.1.call-start = ((), (), s32[]{:S(2)}) async-start(), calls=%async_computation.7 | async-start | bytes 2162688
  399.9 0.8 copy-start.1
Sparse Core Ops, SparseCore 0:
  10.7 74.1 all-gather.1
  397.4 216.6 all-reduce.1
  616.8 122.9 reduce-scatter.3
where the time goes:
time: 754 us; the launch traced here: 749 us
  waiting for transfers between devices  474 us (63%)
  local copies, waits for them, and re-layouts  79.3 us (11%)
  matrix products  78 us (10%)
  starting transfers between devices  72.2 us (10%)
  other arithmetic  23.6 us (3%)
  between operations  21.3 us (3%)
    psum x1, waiting for transfers between devices, on_device(): probe_grad = lax.psum(probe_sum, 'scan')  169 us
    unnamed x4, waiting for transfers between devices  124 us
    ppermute x10, waiting for transfers between devices, from_behind(): return lax.ppermute(block, axis, route)  98.4 us
    dot_general x16, matrix products, contract(): jnp.einsum(form, left_side, right_side, precision=lax.Precision.HIGHEST,...  78 us
    all_gather x1, waiting for transfers between devices, on_device(): band_rows = lax.all_gather(object_slice, 'scan', axis=3, tiled=True)  73 us
    ppermute x10, starting transfers between devices, from_behind(): return lax.ppermute(block, axis, route)  41.7 us
    unnamed x26, local copies, waits for them, and re-layouts  26.5 us
    dynamic_update_slice x4, local copies, waits for them, and re-layouts, add_tile(): return lax.dynamic_update_slice(band_now, current + tile_value, corner)  24.7 us
  transfers between devices with their start and end apart: 17, of which 16 were waited for; matrix products, arithmetic and copies ran while one was open for 11% of the time, Pallas kernels for 0%

commit v1 on v0

--- a/solution.py
+++ b/solution.py
@@ -165,7 +165,7 @@
             grad_band, grad_pair[slot_index, 1], second_cycle[slot_index], left_col[slot_index]
         )
     probe_sum = jnp.stack([jnp.sum(term_re, 0), jnp.sum(term_im, 0)])
-    probe_grad = lax.psum(probe_sum, "scan")
+    probe_grad = jnp.sum(lax.all_gather(probe_sum, "scan"), axis=0)
     object_grad = lax.psum_scatter(
         grad_band.reshape(2, cycles, rows_dev, full_width), "scan", scatter_dimension=3, tiled=True
     )

time: 754 us -> 658 us (0.87)
  the two profiles are of different devices: /device:TPU:8 before, /device:TPU:1 now
where the time goes in v1:
time: 658 us; the launch traced here: 653 us
  waiting for transfers between devices  384 us (58%)
  local copies, waits for them, and re-layouts  79.2 us (12%)
  matrix products  78 us (12%)
  starting transfers between devices  64.2 us (10%)
  other arithmetic  25.2 us (4%)
  between operations  21.3 us (3%)
    unnamed x4, waiting for transfers between devices  120 us
    ppermute x10, waiting for transfers between devices, from_behind(): return lax.ppermute(block, axis, route)  111 us
    dot_general x16, matrix products, contract(): jnp.einsum(form, left_side, right_side, precision=lax.Precision.HIGHEST,...  78 us
    all_gather x1, waiting for transfers between devices, on_device(): band_rows = lax.all_gather(object_slice, 'scan', axis=3, tiled=True)  74.3 us
    all_gather x1, waiting for transfers between devices, on_device(): probe_grad = jnp.sum(lax.all_gather(probe_sum, 'scan'), axis=0)  71.9 us
    ppermute x10, starting transfers between devices, from_behind(): return lax.ppermute(block, axis, route)  36.6 us
    unnamed x26, local copies, waits for them, and re-layouts  26.5 us
    dynamic_update_slice x4, local copies, waits for them, and re-layouts, add_tile(): return lax.dynamic_update_slice(band_now, current + tile_value, corner)  24.6 us
  transfers between devices with their start and end apart: 17, of which 16 were waited for; matrix products, arithmetic and copies ran while one was open for 6% of the time, Pallas kernels for 0%

profile of v1, /device:TPU:1, one launch (start us, length us, event | category | flops | bytes accessed | tf_op | source)
XLA Modules:
  0.0 652.7 jit_solution(10508709182147924221)
XLA Ops:
  11.9 74.3 %all-gather.4.cloned.1.call-done = bf16[2,4,32,2048]{2,1,0,3:T(4,128)(2,1)} async-done(((bf16[2,4,32,64]{2,1,0,3:T(4,128)(2,1)}), bf16[2,4,32,2048]{2,1,0,3:T(4,128)(2,1)}) %all-gather.4.cloned.1.call-update) | async-done | bytes 1048592 | tf_op jit(solution)/shard_map/all_gather | solution.py:56
  86.2 5.5 copy.64
  91.8 4.2 while.4
  96.1 4.2 while.3
  100.7 3.1 collective-permute-start
  103.9 9.9 %collective-permute-done = bf16[2,2,2,32,512]{4,2,0,3,1:T(2,128)(2,1)S(1)} collective-permute-done((bf16[2,2,2,32,512]{4,2,0,3,1:T(2,128)(2,1)S(1)}, bf16[2,2,2,32,512]{4,2,0,3,1:T(2,128)(2,1)S(1)}, u32[]{:S(2)}, u32[]{:S(2)}) %collective-permute-start) | collective-permute-done | bytes 262176 | tf_op jit(solution)/shard_map/ppermute | solution.py:13
  116.3 16.1 %collective-permute-done.1 = bf16[2,2,2,32,512]{4,2,0,3,1:T(2,128)(2,1)S(1)} collective-permute-done((bf16[2,2,2,32,512]{4,2,0,3,1:T(2,128)(2,1)S(1)}, bf16[2,2,2,32,512]{4,2,0,3,1:T(2,128)(2,1)S(1)}, u32[]{:S(2)}, u32[]{:S(2)}) %collective-permute-start.1) | collective-permute-done | bytes 262176 | tf_op jit(solution)/shard_map/ppermute | solution.py:13
  135.2 17.0 %collective-permute-done.2 = bf16[2,2,2,32,512]{4,2,0,3,1:T(2,128)(2,1)S(1)} collective-permute-done((bf16[2,2,2,32,512]{4,2,0,3,1:T(2,128)(2,1)S(1)}, bf16[2,2,2,32,512]{4,2,0,3,1:T(2,128)(2,1)S(1)}, u32[]{:S(2)}, u32[]{:S(2)}) %collective-permute-start.2) | collective-permute-done | bytes 262176 | tf_op jit(solution)/shard_map/ppermute | solution.py:13
  154.6 8.4 %collective-permute-done.3 = bf16[2,2,2,32,512]{4,2,0,3,1:T(2,128)(2,1)S(1)} collective-permute-done((bf16[2,2,2,32,512]{4,2,0,3,1:T(2,128)(2,1)S(1)}, bf16[2,2,2,32,512]{4,2,0,3,1:T(2,128)(2,1)S(1)}, u32[]{:S(2)}, u32[]{:S(2)}) %collective-permute-start.3) | collective-permute-done | bytes 262176 | tf_op jit(solution)/shard_map/ppermute | solution.py:13
  165.7 3.5 collective-permute-done.4
  170.6 5.0 fusion.27
  175.6 5.0 fusion.23
  180.6 5.2 fusion.1
  187.3 5.0 all-to-all-start
  192.3 5.0 fusion
  201.2 7.0 %all-to-all-start.1 = ((f32[16,1,2048]{2,1,0:T(1,128)}), f32[16,1,2048]{2,1,0:T(1,128)S(1)}, u32[]{:S(2)}, u32[]{:S(2)}) async-start(f32[16,1,2048]{2,1,0:T(1,128)} %reshape.372), calls=%async_computation.1 | async-start | bytes 262144 | tf_op jit(solution)/shard_map/all_to_all | solution.py:116
  210.7 4.8 fusion.25
  215.5 4.8 fusion.10
  222.2 4.7 convolution_add_fusion.2
  227.0 5.0 convolution_subtract_fusion.2
  231.9 4.8 fusion.7
  236.8 4.8 fusion.20
  241.6 4.8 convolution_subtract_fusion.1
  247.8 9.2 %all-to-all-start.2 = ((f32[16,1,2048]{2,1,0:T(1,128)}), f32[16,1,2048]{2,1,0:T(1,128)S(1)}, u32[]{:S(2)}, u32[]{:S(2)}) async-start(f32[16,1,2048]{2,1,0:T(1,128)} %reshape.376), calls=%async_computation.2 | async-start | bytes 262144 | tf_op jit(solution)/shard_map/all_to_all | solution.py:124
  257.0 4.8 convolution_add_fusion.1
  265.9 6.3 all-to-all-start.3
  274.3 5.0 fusion.18
  283.1 4.8 fusion.15
  287.9 4.8 convolution_add_fusion
  292.7 4.9 fusion.40
  297.8 14.5 %while.5 = (s32[]{:T(128)}, f32[2,2,64,512]{3,1,0,2:T(2,128)S(1)}, s32[2,4]{1,0:T(2,128)S(1)}, f32[2,2,32,512]{3,2,0,1:T(8,128)S(1)}, s32[]{:T(128)}, /*index=5*/s32[4]{0:T(128)S(1)}) while((s32[]{:T(128)}, f32[2,2,64,512]{3,1,0,2:T(2,128)S(1)}, s32[2,4]{1,0:T(2,128)S(1)}, f32[2,2,32,512]{3,2,0,1:T(8,128)S(1)}, s32[]{:T(128)}, ...), condition=%wide.while_cond.2, body=%wide.while_body.2.sunk | while | flops 32797 | bytes 917703 | solution.py:145
  298.5 3.2 and_reduce_fusion.2
  305.7 3.2 and_reduce_fusion.2
  315.3 7.7 %collective-permute-done.5 = f32[2,2,32,512]{3,1,0,2:T(2,128)S(1)} collective-permute-done((f32[2,2,32,512]{3,1,0,2:T(2,128)S(1)}, f32[2,2,32,512]{3,1,0,2:T(2,128)S(1)}, u32[]{:S(2)}, u32[]{:S(2)}) %collective-permute-start.5) | collective-permute-done | bytes 262176 | tf_op jit(solution)/shard_map/ppermute | solution.py:13
  325.7 11.4 %collective-permute-done.6 = f32[2,2,2,32,512]{4,2,0,3,1:T(2,128)S(1)} collective-permute-done((f32[2,2,2,32,512]{4,2,0,3,1:T(2,128)S(1)}, f32[2,2,2,32,512]{4,2,0,3,1:T(2,128)S(1)}, u32[]{:S(2)}, u32[]{:S(2)}) %collective-permute-start.6) | collective-permute-done | bytes 524320 | tf_op jit(solution)/shard_map/ppermute | solution.py:13
  339.4 16.0 %collective-permute-done.7 = f32[2,2,2,32,512]{4,2,0,3,1:T(2,128)S(1)} collective-permute-done((f32[2,2,2,32,512]{4,2,0,3,1:T(2,128)S(1)}, f32[2,2,2,32,512]{4,2,0,3,1:T(2,128)S(1)}, u32[]{:S(2)}, u32[]{:S(2)}) %collective-permute-start.7) | collective-permute-done | bytes 524320 | tf_op jit(solution)/shard_map/ppermute | solution.py:13
  355.9 4.2 collective-permute-start.8
  360.0 17.5 %collective-permute-done.8 = f32[2,2,2,32,512]{4,2,0,3,1:T(2,128)S(1)} collective-permute-done((f32[2,2,2,32,512]{4,2,0,3,1:T(2,128)S(1)}, f32[2,2,2,32,512]{4,2,0,3,1:T(2,128)S(1)}, u32[]{:S(2)}, u32[]{:S(2)}) %collective-permute-start.8) | collective-permute-done | bytes 524320 | tf_op jit(solution)/shard_map/ppermute | solution.py:13
  377.9 14.2 %collective-permute-start.9 = (f32[2,2,2,32,512]{4,2,0,3,1:T(2,128)S(1)}, f32[2,2,2,32,512]{4,2,0,3,1:T(2,128)S(1)}, u32[]{:S(2)}, u32[]{:S(2)}) collective-permute-start(f32[2,2,2,32,512]{4,2,0,3,1:T(2,128)S(1)} %broadcast_select_fusion.2), channel_id=1, source_target_pairs={{256,0},{288,32},{320,64},{352,96},{384,128},{416,160},{448,192},{... | collective-permute-start | bytes 1572872 | tf_op jit(solution)/shard_map/ppermute | solution.py:13
  399.7 3.8 collective-permute-done.9
  405.7 6.1 dynamic_update_slice.12
  413.0 6.1 dynamic_update_slice.13
  420.3 6.1 dynamic_update_slice.14
  427.6 6.1 dynamic_update_slice.15
  433.7 6.1 copy.84
  439.8 8.6 %reshape.366 = f32[2048,256]{1,0:T(8,128)} reshape(f32[2048,2,4,32]{3,2,1,0:T(4,128)} %bitcast.196) | data formatting | bytes 4194304
  449.2 119.7 %reduce-scatter.4.cloned.1.call-done = f32[64,256]{1,0:T(8,128)} async-done(((f32[2048,256]{1,0:T(8,128)}), f32[64,256]{1,0:T(8,128)}) %reduce-scatter.4.cloned.1.call-update) | async-done | bytes 65552
  570.7 71.9 %all-gather.6.cloned.1.call-done = f32[64,32,512]{2,1,0:T(8,128)} async-done(((f32[2,32,512]{2,1,0:T(8,128)}), f32[64,32,512]{2,1,0:T(8,128)}) %all-gather.6.cloned.1.call-update) | async-done | bytes 4194320 | tf_op jit(solution)/shard_map/all_gather | solution.py:168
  (132 shorter events, 75.6 us)
Async XLA Ops:
  7.2 109.1 %copy-start = (bf16[2,512,512]{2,1,0:T(8,128)(2,1)S(1)}, bf16[2,512,512]{2,1,0:T(8,128)(2,1)}, u32[]{:S(2)}) copy-start(bf16[2,512,512]{2,1,0:T(8,128)(2,1)} %param.6) | copy-start | bytes 3145732
  7.2 79.1 %all-gather.4.cloned.1.call-start = ((), (), s32[]{:S(2)}) async-start(), calls=%async_computation.5 | async-start | bytes 4325376 | tf_op jit(solution)/shard_map/all_gather | solution.py:56
  100.7 13.1 %collective-permute-start = (bf16[2,2,2,32,512]{4,2,0,3,1:T(2,128)(2,1)S(1)}, bf16[2,2,2,32,512]{4,2,0,3,1:T(2,128)(2,1)S(1)}, u32[]{:S(2)}, u32[]{:S(2)}) collective-permute-start(bf16[2,2,2,32,512]{4,2,0,3,1:T(2,128)(2,1)S(1)} %pad_maximum_fusion.1), channel_id=1, source_target_pairs={{480,0},{0,32},{32,64},{64,96},{96,128},{128,160},{160,192},{192,2... | collective-permute-start | bytes 786440 | tf_op jit(solution)/shard_map/ppermute | solution.py:13
  114.3 18.1 %collective-permute-start.1 = (bf16[2,2,2,32,512]{4,2,0,3,1:T(2,128)(2,1)S(1)}, bf16[2,2,2,32,512]{4,2,0,3,1:T(2,128)(2,1)S(1)}, u32[]{:S(2)}, u32[]{:S(2)}) collective-permute-start(bf16[2,2,2,32,512]{4,2,0,3,1:T(2,128)(2,1)S(1)} %broadcast_select_fusion.4), channel_id=1, source_target_pairs={{448,0},{480,32},{0,64},{32,96},{64,128},{96,160},{128,192},{160,2... | collective-permute-start | bytes 786440 | tf_op jit(solution)/shard_map/ppermute | solution.py:13
  133.0 19.3 %collective-permute-start.2 = (bf16[2,2,2,32,512]{4,2,0,3,1:T(2,128)(2,1)S(1)}, bf16[2,2,2,32,512]{4,2,0,3,1:T(2,128)(2,1)S(1)}, u32[]{:S(2)}, u32[]{:S(2)}) collective-permute-start(bf16[2,2,2,32,512]{4,2,0,3,1:T(2,128)(2,1)S(1)} %broadcast_select_fusion.5), channel_id=1, source_target_pairs={{384,0},{416,32},{448,64},{480,96},{0,128},{32,160},{64,192},{96,2... | collective-permute-start | bytes 786440 | tf_op jit(solution)/shard_map/ppermute | solution.py:13
  152.6 10.4 %collective-permute-start.3 = (bf16[2,2,2,32,512]{4,2,0,3,1:T(2,128)(2,1)S(1)}, bf16[2,2,2,32,512]{4,2,0,3,1:T(2,128)(2,1)S(1)}, u32[]{:S(2)}, u32[]{:S(2)}) collective-permute-start(bf16[2,2,2,32,512]{4,2,0,3,1:T(2,128)(2,1)S(1)} %broadcast_select_fusion.6), channel_id=1, source_target_pairs={{256,0},{288,32},{320,64},{352,96},{384,128},{416,160},{448,192},{... | collective-permute-start | bytes 786440 | tf_op jit(solution)/shard_map/ppermute | solution.py:13
  163.5 5.7 collective-permute-start.4
  187.3 13.9 %all-to-all-start = ((f32[16,1,2048]{2,1,0:T(1,128)}), f32[16,1,2048]{2,1,0:T(1,128)S(1)}, u32[]{:S(2)}, u32[]{:S(2)}) async-start(f32[16,1,2048]{2,1,0:T(1,128)} %reshape.370), calls=%async_computation | async-start | bytes 262144 | tf_op jit(solution)/shard_map/all_to_all | solution.py:115
  201.2 19.0 %all-to-all-start.1 = ((f32[16,1,2048]{2,1,0:T(1,128)}), f32[16,1,2048]{2,1,0:T(1,128)S(1)}, u32[]{:S(2)}, u32[]{:S(2)}) async-start(f32[16,1,2048]{2,1,0:T(1,128)} %reshape.372), calls=%async_computation.1 | async-start | bytes 262144 | tf_op jit(solution)/shard_map/all_to_all | solution.py:116
  227.0 5.0 copy-start.3
  247.8 18.1 %all-to-all-start.2 = ((f32[16,1,2048]{2,1,0:T(1,128)}), f32[16,1,2048]{2,1,0:T(1,128)S(1)}, u32[]{:S(2)}, u32[]{:S(2)}) async-start(f32[16,1,2048]{2,1,0:T(1,128)} %reshape.376), calls=%async_computation.2 | async-start | bytes 262144 | tf_op jit(solution)/shard_map/all_to_all | solution.py:124
  265.9 15.3 %all-to-all-start.3 = ((f32[16,1,2048]{2,1,0:T(1,128)}), f32[16,1,2048]{2,1,0:T(1,128)S(1)}, u32[]{:S(2)}, u32[]{:S(2)}) async-start(f32[16,1,2048]{2,1,0:T(1,128)} %reshape.374), calls=%async_computation.3 | async-start | bytes 262144 | tf_op jit(solution)/shard_map/all_to_all | solution.py:125
  272.2 296.6 %reduce-scatter.4.cloned.1.call-start = ((), (), s32[]{:S(2)}) async-start(), calls=%async_computation.7 | async-start | bytes 2162688
  292.7 5.2 copy-start.2
  312.3 10.7 %collective-permute-start.5 = (f32[2,2,32,512]{3,1,0,2:T(2,128)S(1)}, f32[2,2,32,512]{3,1,0,2:T(2,128)S(1)}, u32[]{:S(2)}, u32[]{:S(2)}) collective-permute-start(f32[2,2,32,512]{3,1,0,2:T(2,128)S(1)} %slice.75), channel_id=1, source_target_pairs={{480,0},{0,32},{32,64},{64,96},{96,128},{128,160},{160,192},{192,2... | collective-permute-start | bytes 786440 | tf_op jit(solution)/shard_map/ppermute | solution.py:13
  323.5 13.5 %collective-permute-start.6 = (f32[2,2,2,32,512]{4,2,0,3,1:T(2,128)S(1)}, f32[2,2,2,32,512]{4,2,0,3,1:T(2,128)S(1)}, u32[]{:S(2)}, u32[]{:S(2)}) collective-permute-start(f32[2,2,2,32,512]{4,2,0,3,1:T(2,128)S(1)} %pad_maximum_fusion), channel_id=1, source_target_pairs={{480,0},{0,32},{32,64},{64,96},{96,128},{128,160},{160,192},{192,2... | collective-permute-start | bytes 1572872 | tf_op jit(solution)/shard_map/ppermute | solution.py:13
  337.4 17.9 %collective-permute-start.7 = (f32[2,2,2,32,512]{4,2,0,3,1:T(2,128)S(1)}, f32[2,2,2,32,512]{4,2,0,3,1:T(2,128)S(1)}, u32[]{:S(2)}, u32[]{:S(2)}) collective-permute-start(f32[2,2,2,32,512]{4,2,0,3,1:T(2,128)S(1)} %broadcast_select_fusion), channel_id=1, source_target_pairs={{448,0},{480,32},{0,64},{32,96},{64,128},{96,160},{128,192},{160,2... | collective-permute-start | bytes 1572872 | tf_op jit(solution)/shard_map/ppermute | solution.py:13
  355.9 21.7 %collective-permute-start.8 = (f32[2,2,2,32,512]{4,2,0,3,1:T(2,128)S(1)}, f32[2,2,2,32,512]{4,2,0,3,1:T(2,128)S(1)}, u32[]{:S(2)}, u32[]{:S(2)}) collective-permute-start(f32[2,2,2,32,512]{4,2,0,3,1:T(2,128)S(1)} %broadcast_select_fusion.1), channel_id=1, source_target_pairs={{384,0},{416,32},{448,64},{480,96},{0,128},{32,160},{64,192},{96,2... | collective-permute-start | bytes 1572872 | tf_op jit(solution)/shard_map/ppermute | solution.py:13
  377.9 25.6 %collective-permute-start.9 = (f32[2,2,2,32,512]{4,2,0,3,1:T(2,128)S(1)}, f32[2,2,2,32,512]{4,2,0,3,1:T(2,128)S(1)}, u32[]{:S(2)}, u32[]{:S(2)}) collective-permute-start(f32[2,2,2,32,512]{4,2,0,3,1:T(2,128)S(1)} %broadcast_select_fusion.2), channel_id=1, source_target_pairs={{256,0},{288,32},{320,64},{352,96},{384,128},{416,160},{448,192},{... | collective-permute-start | bytes 1572872 | tf_op jit(solution)/shard_map/ppermute | solution.py:13
  403.9 0.8 copy-start.1
  448.4 194.1 %all-gather.6.cloned.1.call-start = ((), (), s32[]{:S(2)}) async-start(), calls=%async_computation.6 | async-start | bytes 4325376 | tf_op jit(solution)/shard_map/all_gather | solution.py:168
Sparse Core Ops, SparseCore 0:
  10.7 75.4 all-gather.3
  448.5 120.2 reduce-scatter.3
  571.6 70.9 all-gather.5
